TPU v7x, 512 devices: a whole 4x8x8 slice. The times are simulated.
512 devices in a mesh: ta: 32 (over y, x), pb: 16 (over z, core).
Axes of the slice: x: 4, y: 8, z: 8, core: 2. Of those that a mesh axis runs over, the one named last changes fastest.
Arguments:
- particles: float32 [2, 2097152], P(None, ('ta', 'pb')), may hold values from -6 to 6
- weights: bfloat16 [2097152], P(('ta', 'pb')), may hold values from 0.5 to 2
- cell_index: int32 [2097152], P(('ta', 'pb')), may hold values from 0 to 9215
- target_group: int32 [2097152, 1], P(('ta', 'pb')), may hold values from 0 to 31; in each aligned block of 4096 rows (0 to 4095, 4096 to 8191, ...) at most 256 rows name the same one
- target_slice: int32 [2097152], P(('ta', 'pb')), may hold values from 0 to 3
- laser_x: float32 [96], replicated, may hold values from 0.3 to 1.5
- laser_y: float32 [96], replicated, may hold values from 0.3 to 1.5
- mode_x: float32 [96], replicated, may hold values from 0.3 to 1.5
- mode_y: float32 [96], replicated, may hold values from 0.3 to 1.5
- along_coeff: float32 [96, 96], replicated, may hold values from 0.2 to 2
- across_coeff: float32 [96, 96], replicated, may hold values from 0.1 to 1
Outputs:
- arrivals: float32 [2, 4194304], P(None, ('ta', 'pb'))
- radiation: float32 [2, 128], P(None, 'ta')
Inputs may be any that keep to these rules, and one draw needn't show every extreme that they name: `target_group`: in the rows of one device at most 256 rows name the same group, and in every draw some group is named by exactly 256 rows of some device.
All inputs are finite; a program needn't handle non-finite values.
Results may differ from a plain program's by a relative error of at most 0.0009.
Values sent between devices are 32-bit elements; how exact they have to be, the bound alone decides.
No kernel may reach another device: no remote copies, remote signals or barrier semaphores. Data moves between devices by JAX's collectives and lax.ppermute only.
A program may use at most 64 MiB of HBM per device.

v0:
```python
import math
import jax
import jax.numpy as jnp
from jax import lax
from jax.sharding import PartitionSpec as P

SL_DEV = 4
PS_DEV = 1024
HARM = 48
PERIODS = 2
DISPERSION = 3.0
LASER_GAIN = 1.0
KICK_GAIN = 0.5
SLIP_GAIN = 0.05


def with_halo(x, sides, width):
    for axis, dim in sides:
        peers, length = (lax.axis_size(axis), x.shape[dim])
        up = [(i, (i + 1) % peers) for i in range(peers - 1)]
        down = [(j, i) for i, j in up]
        last = lax.slice_in_dim(x, length - width, length, axis=dim)
        leading = lax.slice_in_dim(x, 0, width, axis=dim)
        before = lax.ppermute(last, axis, up)
        after = lax.ppermute(leading, axis, down)
        x = jnp.concatenate([before, x, after], axis=dim)
    return x


def shifted(value, axis, steps):
    count = lax.axis_size(axis)
    leading, last = (max(0, -steps), min(count, count - steps))
    return lax.ppermute(value, axis, [(source, source + steps) for source in range(leading, last)])


def lookup(values_table, positions):
    matches = positions[None, :] == jnp.arange(values_table.shape[0], dtype=jnp.int32)[:, None]
    return jnp.sum(jnp.where(matches, values_table[:, None], 0.0), axis=0)


def arrival_slots(destination, groups):
    count = destination.shape[0]
    block_size = math.gcd(count, 512)
    turn_count = count // block_size
    onehot = (destination[:, None] == jnp.arange(groups, dtype=jnp.int32)[None, :]).astype(
        jnp.bfloat16
    )
    onehot = onehot.reshape(turn_count, block_size, groups)
    earlier = (jnp.arange(block_size)[:, None] > jnp.arange(block_size)[None, :]).astype(
        jnp.bfloat16
    )

    def count_step(counted, onehot_rows):
        before = (
            jnp.dot(earlier, onehot_rows, preferred_element_type=jnp.float32) + counted[None, :]
        )
        rows_f = onehot_rows.astype(jnp.float32)
        return (counted + jnp.sum(rows_f, axis=0), jnp.sum(before * rows_f, axis=1))

    _, arrival = lax.scan(count_step, jnp.zeros((groups,), jnp.float32), onehot)
    return arrival.reshape(count).astype(jnp.int32)


def deposit(arrived_weight, got_slice, got_cell, slice_count, grid_x, grid_y):
    slot_count = arrived_weight.shape[0]
    block_size = math.gcd(slot_count, 2048)
    turn_count = slot_count // block_size
    block_items = (
        arrived_weight.reshape(turn_count, block_size),
        got_slice.reshape(turn_count, block_size),
        got_cell.reshape(turn_count, block_size),
    )

    def deposit_step(running, items):
        block_weight, block_slice, block_cell = items
        on_slice = block_slice[None, :] == jnp.arange(slice_count, dtype=jnp.int32)[:, None]
        on_row = (block_cell // grid_y)[None, :] == jnp.arange(grid_x, dtype=jnp.int32)[:, None]
        left = jnp.where(
            on_slice[:, None, :] & on_row[None, :, :],
            block_weight[None, None, :],
            jnp.zeros((), jnp.bfloat16),
        )
        left = left.reshape(slice_count * grid_x, block_size)
        right = (
            (block_cell % grid_y)[:, None] == jnp.arange(grid_y, dtype=jnp.int32)[None, :]
        ).astype(jnp.bfloat16)
        return (running + jnp.dot(left, right, preferred_element_type=jnp.float32), None)

    running, _ = lax.scan(
        deposit_step, jnp.zeros((slice_count * grid_x, grid_y), jnp.float32), block_items
    )
    return running.reshape(slice_count, grid_x * grid_y)


def stencil(extended, sideways, coeff_long, coeff_cross, grid_y):
    centre = sideways[:, grid_y:-grid_y]
    along_diff = extended[2:] - extended[:-2]
    across = sideways[:, 2 * grid_y :] + sideways[:, : -2 * grid_y]
    column = jnp.arange(centre.shape[1], dtype=jnp.int32) % grid_y
    upper_y = jnp.where(column < grid_y - 1, jnp.pad(centre, ((0, 0), (0, 1)))[:, 1:], 0.0)
    lower_y = jnp.where(column > 0, jnp.pad(centre, ((0, 0), (1, 0)))[:, :-1], 0.0)
    return coeff_long[None, :] * along_diff + coeff_cross[None, :] * (
        4.0 * centre - across - upper_y - lower_y
    )


def body(
    particles,
    weights,
    cell_index,
    target_group,
    target_slice,
    laser_x,
    laser_y,
    mode_x,
    mode_y,
    along_coeff,
    across_coeff,
):
    groups = lax.axis_size("ta")
    splits = lax.axis_size("pb")
    grid_x = laser_x.shape[0]
    grid_y = laser_y.shape[0]
    cell_count = grid_x * grid_y
    per_device = particles.shape[1]
    capacity = 2 * per_device // groups
    slot_count = groups * capacity
    row_x = cell_index // grid_y
    row_y = cell_index % grid_y
    energy = particles[1] + LASER_GAIN * lookup(laser_x, row_x) * lookup(laser_y, row_y) * jnp.sin(
        particles[0]
    )
    phases = particles[0] + DISPERSION * energy
    destination = target_group[:, 0]
    position = destination * capacity + arrival_slots(destination, groups)
    send_float = (
        jnp.zeros((3, slot_count), jnp.float32)
        .at[:, position]
        .set(jnp.stack([phases, energy, weights.astype(jnp.float32)]))
    )
    send_index = (
        jnp.zeros((1, slot_count), jnp.int32)
        .at[0, position]
        .set(target_slice * cell_count + cell_index)
    )
    got_float, got_index = (
        lax.all_to_all(
            send_float.reshape(3, groups, capacity), "ta", split_axis=1, concat_axis=1, tiled=True
        ),
        lax.all_to_all(
            send_index.reshape(1, groups, capacity), "ta", split_axis=1, concat_axis=1, tiled=True
        ),
    )
    got_float = got_float.reshape(3, slot_count)
    combined = got_index.reshape(slot_count)
    arrived_weight = got_float[2]
    got_slice = combined // cell_count
    got_cell = combined % cell_count
    partial_value = deposit(
        arrived_weight.astype(jnp.bfloat16), got_slice, got_cell, SL_DEV, grid_x, grid_y
    )
    long_flat = along_coeff.reshape(cell_count)
    cross_flat = across_coeff.reshape(cell_count)
    summed = lax.psum(partial_value, "pb")
    extended = with_halo(summed, (("ta", 0),), 1)
    sideways = jnp.pad(extended[1:-1], ((0, 0), (grid_y, grid_y)))
    force_map = stencil(extended, sideways, long_flat, cross_flat, grid_y)
    kicked = got_float[1] + jnp.take(force_map.reshape(-1), combined)
    got_phase = got_float[0]
    profile = lookup(mode_x, got_cell // grid_y) * lookup(mode_y, got_cell % grid_y)
    weighted = arrived_weight * profile
    select = (got_slice[None, :] == jnp.arange(SL_DEV, dtype=jnp.int32)[:, None]).astype(
        jnp.float32
    )
    couple = 1.0 / math.sqrt(splits * PS_DEV)
    radiation = jnp.zeros((2, SL_DEV), jnp.float32)
    for period in range(PERIODS):
        harmonic_phase = HARM * got_phase
        cosine = jnp.cos(harmonic_phase)
        sine_part = jnp.sin(harmonic_phase)
        local_sums = jnp.stack(
            [
                jnp.sum(select * (weighted * cosine)[None, :], axis=1),
                jnp.sum(select * (-weighted * sine_part)[None, :], axis=1),
            ]
        )
        bunching = lax.psum(local_sums, "pb")
        radiation = radiation + couple * bunching
        real_here = jnp.sum(select * radiation[0][:, None], axis=0)
        imag_here = jnp.sum(select * radiation[1][:, None], axis=0)
        kicked = kicked + KICK_GAIN * profile * (real_here * cosine - imag_here * sine_part)
        got_phase = got_phase + SLIP_GAIN * kicked
        incoming = shifted(radiation[:, -1:], "ta", 1)
        radiation = jnp.concatenate([incoming, radiation[:, :-1]], axis=1)
    filled = arrived_weight > 0
    result = jnp.stack([jnp.where(filled, got_phase, 0.0), jnp.where(filled, kicked, 0.0)])
    return (result, radiation)


def solution(mesh):
    return jax.shard_map(
        body,
        mesh=mesh,
        in_specs=(
            P(None, ("ta", "pb")),
            P(("ta", "pb")),
            P(("ta", "pb")),
            P(("ta", "pb"), None),
            P(("ta", "pb")),
            P(),
            P(),
            P(),
            P(),
            P(),
            P(),
        ),
        out_specs=(P(None, ("ta", "pb")), P(None, "ta")),
        check_vma=False,
    )
```

profile of v0, /device:TPU:32, one launch (start us, length us, event | category | flops | bytes accessed | tf_op | source)
XLA Modules:
  0.0 320.8 jit_solution(3291533808186617567)
XLA Ops:
  7.8 1.4 reduce.17
  9.3 4.0 %while.26 = (s32[]{:T(128)}, f32[32]{0:T(128)S(1)}, f32[8,512]{1,0:T(8,128)S(1)}, bf16[8,512,32]{1,2,0:T(8,128)(2,1)S(1)}, s32[]{:T(128)}, /*index=5*/s32[]{:T(128)}) while((s32[]{:T(128)}, f32[32]{0:T(128)S(1)}, f32[8,512]{1,0:T(8,128)S(1)}, bf16[8,512,32]{1,2,0:T(8,128)(2,1)S(1)}, s32[]{:T(128)}, /*index=5*/s32[]{:T(128)}) %tuple.81), condition=%wide.region_3.4_spmd.clone, body=%wide.region_0.3_spmd.clone.sunk | while | flops 17399332 | bytes 106719 | solution.py:60
  13.7 16.1 %scatter_custom_fusion.1 = s32[8192]{0:T(1024)} fusion(s32[4096]{0:T(1024)S(1)} %broadcast_select_fusion.2, s32[4096]{0:T(1024)S(1)} %get-tuple-element.186, s32[]{:T(128)} %constant.147.clone.1), kind=kCustom, calls=%fused_computation.109 | custom fusion | bytes 32772
  29.8 9.8 %all-to-all-start.1 = ((s32[1,32,256]{2,0,1:T(1,128)}), s32[1,32,256]{2,0,1:T(1,128)S(1)}, u32[]{:S(2)}, u32[]{:S(2)}) async-start(s32[1,32,256]{2,0,1:T(1,128)} %bitcast.8), calls=%async_computation.1 | async-start | bytes 65536 | tf_op jit(solution)/shard_map/all_to_all | solution.py:150
  39.7 0.5 select_reduce_fusion.2
  40.8 0.6 copy.23
  41.4 12.8 %scatter_custom_fusion = f32[3,8192]{0,1:T(8,128)} fusion(s32[4096]{0:T(1024)S(1)} %bitcast.101, f32[4096,3]{1,0:T(8,128)S(1)} %copy.23, f32[]{:T(128)} %constant.145.clone.1), kind=kCustom, calls=%fused_computation.31 | custom fusion | bytes 98308 | tf_op jit(solution)/shard_map/scatter | solution.py:139
  54.2 3.5 %copy.24 = f32[3,32,256]{2,0,1:T(4,128)} copy(f32[3,32,256]{0,2,1:T(8,128)} %bitcast.82) | data formatting | bytes 196608 | tf_op jit(solution)/shard_map/reshape | solution.py:148
  57.9 9.8 %all-to-all-start = ((f32[3,32,256]{2,0,1:T(4,128)}), f32[3,32,256]{2,0,1:T(4,128)S(1)}, u32[]{:S(2)}, u32[]{:S(2)}) async-start(f32[3,32,256]{2,0,1:T(4,128)} %copy.24), calls=%async_computation | async-start | bytes 262144 | tf_op jit(solution)/shard_map/all_to_all | solution.py:147
  68.4 1.0 select_reduce_fusion
  69.4 4.2 %all-to-all-done = f32[3,32,256]{2,0,1:T(4,128)S(1)} async-done(((f32[3,32,256]{2,0,1:T(4,128)}), f32[3,32,256]{2,0,1:T(4,128)S(1)}, u32[]{:S(2)}, u32[]{:S(2)}) %all-to-all-start) | async-done | bytes 98336 | tf_op jit(solution)/shard_map/all_to_all | solution.py:147
  74.2 30.3 %psum.22 = f32[2,4]{1,0:T(2,128)S(1)} all-reduce(f32[2,4]{1,0:T(2,128)S(1)} %pad_maximum_fusion.3), channel_id=1, replica_groups=mesh['ta'=32,'pb'=16] {'pb'}, use_global_device_ids=true, to_apply=%region_15.16 | all-reduce | flops 8 | bytes 64 | tf_op jit(solution)/shard_map/psum | solution.py:187
  104.6 8.0 %while.27 = (s32[]{:T(128)}, f32[384,96]{0,1:T(8,128)S(1)}, s32[4,2048]{1,0:T(4,128)S(1)}, s32[4,2048]{1,0:T(4,128)S(1)}, bf16[4,2048]{1,0:T(4,128)(2,1)S(1)}, /*index=5*/s32[]{:T(128)}, s32[]{:T(128)}) while((s32[]{:T(128)}, f32[384,96]{0,1:T(8,128)S(1)}, s32[4,2048]{1,0:T(4,128)S(1)}, s32[4,2048]{1,0:T(4,128)S(1)}, ...), condition=%wide.region_9.10_spmd.clone, body=%wide.region_8.9_spmd.clone.sunk | while | flops 153069568 | bytes 5517415 | solution.py:89
  105.6 1.0 convolution_add_fusion.3
  107.6 1.0 convolution_add_fusion.3
  109.6 1.0 convolution_add_fusion.3
  111.6 1.0 convolution_add_fusion.3
  112.8 0.8 reshape.556
  113.7 2.5 collective-permute-start.2
  116.2 101.6 %all-reduce.6.cloned.1.call-done = f32[4,9216]{1,0:T(4,128)} async-done(((f32[4,9216]{1,0:T(4,128)}), f32[4,9216]{1,0:T(4,128)}) %all-reduce.6.cloned.1.call-update) | async-done | bytes 147472 | tf_op jit(solution)/shard_map/psum | solution.py:164
  217.9 1.0 fusion.37
  218.9 3.4 %collective-permute-start.1 = (f32[1,9216]{1,0:T(1,128)S(1)}, f32[1,9216]{1,0:T(1,128)S(1)}, u32[]{:S(2)}, u32[]{:S(2)}) collective-permute-start(f32[1,9216]{1,0:T(1,128)S(1)} %get-tuple-element.177), channel_id=1, source_target_pairs={{0,16},{16,32},{32,48},{48,64},{64,80},{80,96},{96,112},{112,128},... | collective-permute-start | bytes 110600 | tf_op jit(solution)/shard_map/ppermute | solution.py:24
  222.3 6.0 %collective-permute-start = (f32[1,9216]{1,0:T(1,128)S(1)}, f32[1,9216]{1,0:T(1,128)S(1)}, u32[]{:S(2)}, u32[]{:S(2)}) collective-permute-start(f32[1,9216]{1,0:T(1,128)S(1)} %get-tuple-element.176), channel_id=1, source_target_pairs={{16,0},{32,16},{48,32},{64,48},{80,64},{96,80},{112,96},{128,112},... | collective-permute-start | bytes 110600 | tf_op jit(solution)/shard_map/ppermute | solution.py:25
  228.5 1.2 collective-permute-done
  229.7 2.0 fusion.19
  231.8 45.5 %gather_fusion = f32[8192]{0:T(1024)S(1)} fusion(f32[36864]{0:T(1024)S(1)} %bitcast.81, s32[8192]{0:T(1024)S(1)} %broadcast_clamp_fusion), kind=kCustom, calls=%fused_computation | custom fusion | bytes 98304 | tf_op jit(solution)/shard_map/jit(_take)/gather | solution.py:168
  278.0 23.5 %psum.23 = f32[2,4]{1,0:T(2,128)S(1)} all-reduce(f32[2,4]{1,0:T(2,128)S(1)} %pad_maximum_fusion.4), channel_id=1, replica_groups=mesh['ta'=32,'pb'=16] {'pb'}, use_global_device_ids=true, to_apply=%region_20.21 | all-reduce | flops 8 | bytes 64 | tf_op jit(solution)/shard_map/psum | solution.py:187
  301.9 2.2 add_select_fusion.8
  304.3 1.9 collective-permute-start.3
  306.2 0.7 pad_maximum_fusion.2
  306.9 6.5 %collective-permute-done.3 = f32[2,1]{1,0:T(2,128)S(1)} collective-permute-done((f32[2,1]{1,0:T(2,128)S(1)}, f32[2,1]{1,0:T(2,128)S(1)}, u32[]{:S(2)}, u32[]{:S(2)}) %collective-permute-start.3) | collective-permute-done | bytes 40 | tf_op jit(solution)/shard_map/ppermute | solution.py:33
  313.4 0.6 pad_maximum_fusion.5
  (143 shorter events, 11.9 us)
Async XLA Ops:
  7.2 6.2 %copy-start.12 = (s32[2]{0:T(128)S(1)}, s32[2]{0:T(128)}, u32[]{:S(2)}) copy-start(s32[2]{0:T(128)} %constant.174) | copy-start | bytes 28
  7.2 6.3 %copy-start.11 = (s32[2]{0:T(128)S(1)}, s32[2]{0:T(128)}, u32[]{:S(2)}) copy-start(s32[2]{0:T(128)} %constant.171) | copy-start | bytes 28
  7.2 6.1 %copy-start = (s32[4096,1]{0,1:T(1,128)S(1)}, s32[4096,1]{0,1:T(1,128)}, u32[]{:S(2)}) copy-start(s32[4096,1]{0,1:T(1,128)} %param.18) | copy-start | bytes 49156
  7.2 6.4 %copy-start.4 = (s32[4096]{0:T(1024)S(1)}, s32[4096]{0:T(1024)}, u32[]{:S(2)}) copy-start(s32[4096]{0:T(1024)} %param.17) | copy-start | bytes 49156
  7.2 6.4 %copy-start.5 = (s32[4096]{0:T(1024)S(1)}, s32[4096]{0:T(1024)}, u32[]{:S(2)}) copy-start(s32[4096]{0:T(1024)} %param.19) | copy-start | bytes 49156
  7.2 32.4 %copy-start.6 = (bf16[4096]{0:T(1024)(128)(2,1)S(1)}, bf16[4096]{0:T(1024)(128)(2,1)}, u32[]{:S(2)}) copy-start(bf16[4096]{0:T(1024)(128)(2,1)} %param.16) | copy-start | bytes 24580
  7.2 32.4 %copy-start.7 = (f32[96]{0:T(128)S(1)}, f32[96]{0:T(128)}, u32[]{:S(2)}) copy-start(f32[96]{0:T(128)} %param.21) | copy-start | bytes 1156
  7.2 32.4 %copy-start.8 = (f32[96]{0:T(128)S(1)}, f32[96]{0:T(128)}, u32[]{:S(2)}) copy-start(f32[96]{0:T(128)} %param.20) | copy-start | bytes 1156
  7.3 33.0 %copy-start.3 = (f32[2,4096]{1,0:T(2,128)S(1)}, f32[2,4096]{1,0:T(2,128)}, u32[]{:S(2)}) copy-start(f32[2,4096]{1,0:T(2,128)} %param.15) | copy-start | bytes 98308
  29.8 28.1 %all-to-all-start.1 = ((s32[1,32,256]{2,0,1:T(1,128)}), s32[1,32,256]{2,0,1:T(1,128)S(1)}, u32[]{:S(2)}, u32[]{:S(2)}) async-start(s32[1,32,256]{2,0,1:T(1,128)} %bitcast.8), calls=%async_computation.1 | async-start | bytes 65536 | tf_op jit(solution)/shard_map/all_to_all | solution.py:150
  54.2 3.5 %copy-start.1 = (f32[96,96]{1,0:T(8,128)S(1)}, f32[96,96]{1,0:T(8,128)}, u32[]{:S(2)}) copy-start(f32[96,96]{1,0:T(8,128)} %param.25) | copy-start | bytes 110596
  54.2 3.6 %copy-start.2 = (f32[96,96]{1,0:T(8,128)S(1)}, f32[96,96]{1,0:T(8,128)}, u32[]{:S(2)}) copy-start(f32[96,96]{1,0:T(8,128)} %param.24) | copy-start | bytes 110596
  54.2 14.2 %copy-start.9 = (f32[96]{0:T(128)S(1)}, f32[96]{0:T(128)}, u32[]{:S(2)}) copy-start(f32[96]{0:T(128)} %param.23) | copy-start | bytes 1156
  54.2 14.2 %copy-start.10 = (f32[96]{0:T(128)S(1)}, f32[96]{0:T(128)}, u32[]{:S(2)}) copy-start(f32[96]{0:T(128)} %param.22) | copy-start | bytes 1156
  57.9 15.7 %all-to-all-start = ((f32[3,32,256]{2,0,1:T(4,128)}), f32[3,32,256]{2,0,1:T(4,128)S(1)}, u32[]{:S(2)}, u32[]{:S(2)}) async-start(f32[3,32,256]{2,0,1:T(4,128)} %copy.24), calls=%async_computation | async-start | bytes 262144 | tf_op jit(solution)/shard_map/all_to_all | solution.py:147
  67.7 150.2 %all-reduce.6.cloned.1.call-start = ((), (), s32[]{:S(2)}) async-start(), calls=%async_computation.2 | async-start | bytes 294912 | tf_op jit(solution)/shard_map/psum | solution.py:164
  113.7 187.8 %collective-permute-start.2 = (f32[2,1]{1,0:T(2,128)S(1)}, f32[2,1]{1,0:T(2,128)S(1)}, u32[]{:S(2)}, u32[]{:S(2)}) collective-permute-start(f32[2,1]{1,0:T(2,128)S(1)} %slice.85), channel_id=1, source_target_pairs={{0,16},{16,32},{32,48},{48,64},{64,80},{80,96},{96,112},{112,128},... | collective-permute-start | bytes 32 | tf_op jit(solution)/shard_map/ppermute | solution.py:33
  218.9 9.6 %collective-permute-start.1 = (f32[1,9216]{1,0:T(1,128)S(1)}, f32[1,9216]{1,0:T(1,128)S(1)}, u32[]{:S(2)}, u32[]{:S(2)}) collective-permute-start(f32[1,9216]{1,0:T(1,128)S(1)} %get-tuple-element.177), channel_id=1, source_target_pairs={{0,16},{16,32},{32,48},{48,64},{64,80},{80,96},{96,112},{112,128},... | collective-permute-start | bytes 110600 | tf_op jit(solution)/shard_map/ppermute | solution.py:24
  222.3 7.4 %collective-permute-start = (f32[1,9216]{1,0:T(1,128)S(1)}, f32[1,9216]{1,0:T(1,128)S(1)}, u32[]{:S(2)}, u32[]{:S(2)}) collective-permute-start(f32[1,9216]{1,0:T(1,128)S(1)} %get-tuple-element.176), channel_id=1, source_target_pairs={{16,0},{32,16},{48,32},{64,48},{80,64},{96,80},{112,96},{128,112},... | collective-permute-start | bytes 110600 | tf_op jit(solution)/shard_map/ppermute | solution.py:25
  304.3 9.1 %collective-permute-start.3 = (f32[2,1]{1,0:T(2,128)S(1)}, f32[2,1]{1,0:T(2,128)S(1)}, u32[]{:S(2)}, u32[]{:S(2)}) collective-permute-start(f32[2,1]{1,0:T(2,128)S(1)} %slice.89), channel_id=1, source_target_pairs={{0,16},{16,32},{32,48},{48,64},{64,80},{80,96},{96,112},{112,128},... | collective-permute-start | bytes 32 | tf_op jit(solution)/shard_map/ppermute | solution.py:33
Sparse Core Ops, SparseCore 0:
  113.8 104.0 all-reduce.5
where the time goes:
time: 321 us
  waiting for transfers between devices  114 us (36%)
  local copies, waits for them, and re-layouts  82.4 us (26%)
  blocking collectives  53.8 us (17%)
  starting transfers between devices  33.4 us (10%)
  other arithmetic  16.3 us (5%)
  between operations  14.6 us (5%)
  matrix products  6.37 us (2%)
    psum x1, waiting for transfers between devices, body(): summed = lax.psum(partial_value, 'pb')  102 us
    psum x2, blocking collectives, body(): bunching = lax.psum(local_sums, 'pb')  53.8 us
    gather x1, local copies, waits for them, and re-layouts, body(): kicked = got_float[1] + jnp.take(force_map.reshape(-1), combined)  45.5 us
    unnamed x30, local copies, waits for them, and re-layouts  16.7 us
    scatter x1, local copies, waits for them, and re-layouts, body(): send_float = jnp.zeros((3, slot_count), jnp.float32).at[:, position].set(...  12.8 us
    all_to_all x1, starting transfers between devices, body(): lax.all_to_all(send_index.reshape(1, groups, capacity), 'ta', split_axis=...  9.83 us
    all_to_all x1, starting transfers between devices, body(): lax.all_to_all(send_float.reshape(3, groups, capacity), 'ta', split_axis=...  9.79 us
    ppermute x2, waiting for transfers between devices, shifted(): lax.ppermute(value, axis, [(source, source + steps) for source in range(l...  6.48 us
  transfers between devices with their start and end apart: 7, of which 4 were waited for; matrix products, arithmetic and copies ran while one was open for 22% of the time, Pallas kernels for 0%

commit v1 on v0

--- a/solution.py
+++ b/solution.py
@@ -1,3 +1,4 @@
+import functools
 import math
 import jax
 import jax.numpy as jnp
@@ -12,6 +13,15 @@
 LASER_GAIN = 1.0
 KICK_GAIN = 0.5
 SLIP_GAIN = 0.05
+
+
+def trace_points(buf, lane_axis):
+    e_now = jnp.stack(jnp.split(buf, lax.psum(1, lane_axis), 1), axis=0)
+    current_value = lax.all_to_all(e_now, axis_name=lane_axis, split_axis=0, concat_axis=0)
+    return jnp.concatenate(current_value, axis=1)
+
+
+pages_step_on = functools.partial(trace_points, lane_axis="ta")
 
 
 def with_halo(x, sides, width):
@@ -147,9 +157,7 @@
         lax.all_to_all(
             send_float.reshape(3, groups, capacity), "ta", split_axis=1, concat_axis=1, tiled=True
         ),
-        lax.all_to_all(
-            send_index.reshape(1, groups, capacity), "ta", split_axis=1, concat_axis=1, tiled=True
-        ),
+        pages_step_on(send_index.reshape(1, groups, capacity)),
     )
     got_float = got_float.reshape(3, slot_count)
     combined = got_index.reshape(slot_count)

time: 321 us -> 339 us (1.056)
  local copies, waits for them, and re-layouts: 82.4 us -> 99.9 us
    unnamed x30 -> x61, local copies, waits for them, and re-layouts: 16.7 us -> 33.6 us
  transfers between devices with their start and end apart: 7 -> 7, of which waited for: 4 -> 4; matrix products, arithmetic and copies ran while one was open for 22% -> 21% of each run, Pallas kernels for 0% -> 0%
where the time goes in v1:
time: 339 us; the launch traced here: 338 us
  waiting for transfers between devices  114 us (34%)
  local copies, waits for them, and re-layouts  99.9 us (29%)
  blocking collectives  53.8 us (16%)
  starting transfers between devices  33.4 us (10%)
  other arithmetic  16.3 us (5%)
  between operations  14.6 us (4%)
  matrix products  6.37 us (2%)
    psum x1, waiting for transfers between devices, body(): summed = lax.psum(partial_value, 'pb')  102 us
    psum x2, blocking collectives, body(): bunching = lax.psum(local_sums, 'pb')  53.8 us
    gather x1, local copies, waits for them, and re-layouts, body(): kicked = got_float[1] + jnp.take(force_map.reshape(-1), combined)  45.5 us
    unnamed x61, local copies, waits for them, and re-layouts  33.6 us
    scatter x1, local copies, waits for them, and re-layouts, body(): send_float = jnp.zeros((3, slot_count), jnp.float32).at[:, position].set(...  12.8 us
    all_to_all x1, starting transfers between devices, trace_points(): lax.all_to_all(e_now, axis_name=lane_axis, split_axis=0, concat_axis=0)  9.83 us
    all_to_all x1, starting transfers between devices, body(): lax.all_to_all(send_float.reshape(3, groups, capacity), 'ta', split_axis=...  9.79 us
  transfers between devices with their start and end apart: 7, of which 4 were waited for; matrix products, arithmetic and copies ran while one was open for 21% of the time, Pallas kernels for 0%

profile of v1, /device:TPU:32, one launch (start us, length us, event | category | flops | bytes accessed | tf_op | source)
XLA Modules:
  0.0 338.4 jit_solution(14807000970858624350)
XLA Ops:
  7.8 1.4 reduce.17
  9.3 4.0 %while.26 = (s32[]{:T(128)}, f32[32]{0:T(128)S(1)}, f32[8,512]{1,0:T(8,128)S(1)}, bf16[8,512,32]{1,2,0:T(8,128)(2,1)S(1)}, s32[]{:T(128)}, /*index=5*/s32[]{:T(128)}) while((s32[]{:T(128)}, f32[32]{0:T(128)S(1)}, f32[8,512]{1,0:T(8,128)S(1)}, bf16[8,512,32]{1,2,0:T(8,128)(2,1)S(1)}, s32[]{:T(128)}, /*index=5*/s32[]{:T(128)}) %tuple.81), condition=%wide.region_3.4_spmd.clone, body=%wide.region_0.3_spmd.clone.sunk | while | flops 17399332 | bytes 106719 | solution.py:70
  13.7 15.5 %scatter_custom_fusion.1 = s32[8192]{0:T(1024)S(1)} fusion(s32[4096]{0:T(1024)S(1)} %broadcast_select_fusion.2, s32[4096]{0:T(1024)S(1)} %get-tuple-element.186, s32[]{:T(128)} %constant.147.clone.1), kind=kCustom, calls=%fused_computation.141 | custom fusion | bytes 32772
  29.2 0.6 constant_dynamic-update-slice_fusion.31
  47.3 9.8 %all-to-all-start.1 = ((s32[32,1,1,256]{3,2,1,0:T(1,128)}), s32[32,1,1,256]{3,2,1,0:T(1,128)S(1)}, u32[]{:S(2)}, u32[]{:S(2)}) async-start(s32[32,1,1,256]{3,2,1,0:T(1,128)} %constant_dynamic-update-slice_fusion), calls=%async_computation.1 | async-start | bytes 65536 | tf_op jit(solution)/shard_map/all_to_all | solution.py:20
  58.3 0.6 copy.23
  59.0 12.8 %scatter_custom_fusion = f32[3,8192]{0,1:T(8,128)} fusion(s32[4096]{0:T(1024)S(1)} %bitcast.228, f32[4096,3]{1,0:T(8,128)S(1)} %copy.23, f32[]{:T(128)} %constant.145.clone.1), kind=kCustom, calls=%fused_computation.31 | custom fusion | bytes 98308 | tf_op jit(solution)/shard_map/scatter | solution.py:149
  71.8 3.5 %copy.24 = f32[3,32,256]{2,0,1:T(4,128)} copy(f32[3,32,256]{0,2,1:T(8,128)} %bitcast.209) | data formatting | bytes 196608 | tf_op jit(solution)/shard_map/reshape | solution.py:158
  75.4 9.8 %all-to-all-start = ((f32[3,32,256]{2,0,1:T(4,128)}), f32[3,32,256]{2,0,1:T(4,128)S(1)}, u32[]{:S(2)}, u32[]{:S(2)}) async-start(f32[3,32,256]{2,0,1:T(4,128)} %copy.24), calls=%async_computation | async-start | bytes 262144 | tf_op jit(solution)/shard_map/all_to_all | solution.py:157
  85.9 1.0 select_reduce_fusion
  87.0 4.2 %all-to-all-done = f32[3,32,256]{2,0,1:T(4,128)S(1)} async-done(((f32[3,32,256]{2,0,1:T(4,128)}), f32[3,32,256]{2,0,1:T(4,128)S(1)}, u32[]{:S(2)}, u32[]{:S(2)}) %all-to-all-start) | async-done | bytes 98336 | tf_op jit(solution)/shard_map/all_to_all | solution.py:157
  91.8 30.3 %psum.22 = f32[2,4]{1,0:T(2,128)S(1)} all-reduce(f32[2,4]{1,0:T(2,128)S(1)} %pad_maximum_fusion.3), channel_id=1, replica_groups=mesh['ta'=32,'pb'=16] {'pb'}, use_global_device_ids=true, to_apply=%region_15.16 | all-reduce | flops 8 | bytes 64 | tf_op jit(solution)/shard_map/psum | solution.py:195
  122.2 8.0 %while.27 = (s32[]{:T(128)}, f32[384,96]{0,1:T(8,128)S(1)}, s32[4,2048]{1,0:T(4,128)S(1)}, s32[4,2048]{1,0:T(4,128)S(1)}, bf16[4,2048]{1,0:T(4,128)(2,1)S(1)}, /*index=5*/s32[]{:T(128)}, s32[]{:T(128)}) while((s32[]{:T(128)}, f32[384,96]{0,1:T(8,128)S(1)}, s32[4,2048]{1,0:T(4,128)S(1)}, s32[4,2048]{1,0:T(4,128)S(1)}, ...), condition=%wide.region_9.10_spmd.clone, body=%wide.region_8.9_spmd.clone.sunk | while | flops 153069568 | bytes 5517415 | solution.py:99
  123.1 1.0 convolution_add_fusion.3
  125.1 1.0 convolution_add_fusion.3
  127.1 1.0 convolution_add_fusion.3
  129.2 1.0 convolution_add_fusion.3
  130.3 0.8 reshape.548
  131.3 2.5 collective-permute-start.2
  133.8 101.6 %all-reduce.6.cloned.1.call-done = f32[4,9216]{1,0:T(4,128)} async-done(((f32[4,9216]{1,0:T(4,128)}), f32[4,9216]{1,0:T(4,128)}) %all-reduce.6.cloned.1.call-update) | async-done | bytes 147472 | tf_op jit(solution)/shard_map/psum | solution.py:172
  235.4 1.0 fusion.37
  236.5 3.4 collective-permute-start.1
  239.8 6.0 %collective-permute-start = (f32[1,9216]{1,0:T(1,128)S(1)}, f32[1,9216]{1,0:T(1,128)S(1)}, u32[]{:S(2)}, u32[]{:S(2)}) collective-permute-start(f32[1,9216]{1,0:T(1,128)S(1)} %get-tuple-element.176), channel_id=1, source_target_pairs={{16,0},{32,16},{48,32},{64,48},{80,64},{96,80},{112,96},{128,112},... | collective-permute-start | bytes 110600 | tf_op jit(solution)/shard_map/ppermute | solution.py:35
  246.1 1.2 collective-permute-done
  247.2 2.0 fusion.19
  249.3 45.5 %gather_fusion = f32[8192]{0:T(1024)S(1)} fusion(f32[36864]{0:T(1024)S(1)} %bitcast.208, s32[8192]{0:T(1024)S(1)} %broadcast_clamp_fusion), kind=kCustom, calls=%fused_computation | custom fusion | bytes 98304 | tf_op jit(solution)/shard_map/jit(_take)/gather | solution.py:176
  295.6 23.5 %psum.23 = f32[2,4]{1,0:T(2,128)S(1)} all-reduce(f32[2,4]{1,0:T(2,128)S(1)} %pad_maximum_fusion.4), channel_id=1, replica_groups=mesh['ta'=32,'pb'=16] {'pb'}, use_global_device_ids=true, to_apply=%region_20.21 | all-reduce | flops 8 | bytes 64 | tf_op jit(solution)/shard_map/psum | solution.py:195
  319.5 2.2 add_select_fusion.8
  321.8 1.9 collective-permute-start.3
  323.7 0.7 pad_maximum_fusion.2
  324.4 6.5 %collective-permute-done.3 = f32[2,1]{1,0:T(2,128)S(1)} collective-permute-done((f32[2,1]{1,0:T(2,128)S(1)}, f32[2,1]{1,0:T(2,128)S(1)}, u32[]{:S(2)}, u32[]{:S(2)}) %collective-permute-start.3) | collective-permute-done | bytes 40 | tf_op jit(solution)/shard_map/ppermute | solution.py:43
  330.9 0.6 pad_maximum_fusion.5
  (176 shorter events, 30.0 us)
Async XLA Ops:
  7.2 6.2 %copy-start.12 = (s32[2]{0:T(128)S(1)}, s32[2]{0:T(128)}, u32[]{:S(2)}) copy-start(s32[2]{0:T(128)} %constant.174) | copy-start | bytes 28
  7.2 6.3 %copy-start.11 = (s32[2]{0:T(128)S(1)}, s32[2]{0:T(128)}, u32[]{:S(2)}) copy-start(s32[2]{0:T(128)} %constant.171) | copy-start | bytes 28
  7.2 6.1 %copy-start = (s32[4096,1]{0,1:T(1,128)S(1)}, s32[4096,1]{0,1:T(1,128)}, u32[]{:S(2)}) copy-start(s32[4096,1]{0,1:T(1,128)} %param.18) | copy-start | bytes 49156
  7.2 6.4 %copy-start.4 = (s32[4096]{0:T(1024)S(1)}, s32[4096]{0:T(1024)}, u32[]{:S(2)}) copy-start(s32[4096]{0:T(1024)} %param.17) | copy-start | bytes 49156
  7.2 6.4 %copy-start.5 = (s32[4096]{0:T(1024)S(1)}, s32[4096]{0:T(1024)}, u32[]{:S(2)}) copy-start(s32[4096]{0:T(1024)} %param.19) | copy-start | bytes 49156
  7.2 49.9 %copy-start.6 = (bf16[4096]{0:T(1024)(128)(2,1)S(1)}, bf16[4096]{0:T(1024)(128)(2,1)}, u32[]{:S(2)}) copy-start(bf16[4096]{0:T(1024)(128)(2,1)} %param.16) | copy-start | bytes 24580
  7.2 49.9 %copy-start.7 = (f32[96]{0:T(128)S(1)}, f32[96]{0:T(128)}, u32[]{:S(2)}) copy-start(f32[96]{0:T(128)} %param.21) | copy-start | bytes 1156
  7.2 49.9 %copy-start.8 = (f32[96]{0:T(128)S(1)}, f32[96]{0:T(128)}, u32[]{:S(2)}) copy-start(f32[96]{0:T(128)} %param.20) | copy-start | bytes 1156
  7.3 50.5 %copy-start.3 = (f32[2,4096]{1,0:T(2,128)S(1)}, f32[2,4096]{1,0:T(2,128)}, u32[]{:S(2)}) copy-start(f32[2,4096]{1,0:T(2,128)} %param.15) | copy-start | bytes 98308
  47.3 28.1 %all-to-all-start.1 = ((s32[32,1,1,256]{3,2,1,0:T(1,128)}), s32[32,1,1,256]{3,2,1,0:T(1,128)S(1)}, u32[]{:S(2)}, u32[]{:S(2)}) async-start(s32[32,1,1,256]{3,2,1,0:T(1,128)} %constant_dynamic-update-slice_fusion), calls=%async_computation.1 | async-start | bytes 65536 | tf_op jit(solution)/shard_map/all_to_all | solution.py:20
  71.7 3.5 %copy-start.1 = (f32[96,96]{1,0:T(8,128)S(1)}, f32[96,96]{1,0:T(8,128)}, u32[]{:S(2)}) copy-start(f32[96,96]{1,0:T(8,128)} %param.25) | copy-start | bytes 110596
  71.7 3.6 %copy-start.2 = (f32[96,96]{1,0:T(8,128)S(1)}, f32[96,96]{1,0:T(8,128)}, u32[]{:S(2)}) copy-start(f32[96,96]{1,0:T(8,128)} %param.24) | copy-start | bytes 110596
  71.7 14.2 %copy-start.9 = (f32[96]{0:T(128)S(1)}, f32[96]{0:T(128)}, u32[]{:S(2)}) copy-start(f32[96]{0:T(128)} %param.23) | copy-start | bytes 1156
  71.7 14.2 %copy-start.10 = (f32[96]{0:T(128)S(1)}, f32[96]{0:T(128)}, u32[]{:S(2)}) copy-start(f32[96]{0:T(128)} %param.22) | copy-start | bytes 1156
  75.4 15.7 %all-to-all-start = ((f32[3,32,256]{2,0,1:T(4,128)}), f32[3,32,256]{2,0,1:T(4,128)S(1)}, u32[]{:S(2)}, u32[]{:S(2)}) async-start(f32[3,32,256]{2,0,1:T(4,128)} %copy.24), calls=%async_computation | async-start | bytes 262144 | tf_op jit(solution)/shard_map/all_to_all | solution.py:157
  85.2 150.2 %all-reduce.6.cloned.1.call-start = ((), (), s32[]{:S(2)}) async-start(), calls=%async_computation.2 | async-start | bytes 294912 | tf_op jit(solution)/shard_map/psum | solution.py:172
  131.3 187.8 %collective-permute-start.2 = (f32[2,1]{1,0:T(2,128)S(1)}, f32[2,1]{1,0:T(2,128)S(1)}, u32[]{:S(2)}, u32[]{:S(2)}) collective-permute-start(f32[2,1]{1,0:T(2,128)S(1)} %slice.85), channel_id=1, source_target_pairs={{0,16},{16,32},{32,48},{48,64},{64,80},{80,96},{96,112},{112,128},... | collective-permute-start | bytes 32 | tf_op jit(solution)/shard_map/ppermute | solution.py:43
  236.5 9.6 %collective-permute-start.1 = (f32[1,9216]{1,0:T(1,128)S(1)}, f32[1,9216]{1,0:T(1,128)S(1)}, u32[]{:S(2)}, u32[]{:S(2)}) collective-permute-start(f32[1,9216]{1,0:T(1,128)S(1)} %get-tuple-element.177), channel_id=1, source_target_pairs={{0,16},{16,32},{32,48},{48,64},{64,80},{80,96},{96,112},{112,128},... | collective-permute-start | bytes 110600 | tf_op jit(solution)/shard_map/ppermute | solution.py:34
  239.8 7.4 %collective-permute-start = (f32[1,9216]{1,0:T(1,128)S(1)}, f32[1,9216]{1,0:T(1,128)S(1)}, u32[]{:S(2)}, u32[]{:S(2)}) collective-permute-start(f32[1,9216]{1,0:T(1,128)S(1)} %get-tuple-element.176), channel_id=1, source_target_pairs={{16,0},{32,16},{48,32},{64,48},{80,64},{96,80},{112,96},{128,112},... | collective-permute-start | bytes 110600 | tf_op jit(solution)/shard_map/ppermute | solution.py:35
  321.8 9.1 %collective-permute-start.3 = (f32[2,1]{1,0:T(2,128)S(1)}, f32[2,1]{1,0:T(2,128)S(1)}, u32[]{:S(2)}, u32[]{:S(2)}) collective-permute-start(f32[2,1]{1,0:T(2,128)S(1)} %slice.89), channel_id=1, source_target_pairs={{0,16},{16,32},{32,48},{48,64},{64,80},{80,96},{96,112},{112,128},... | collective-permute-start | bytes 32 | tf_op jit(solution)/shard_map/ppermute | solution.py:43
Sparse Core Ops, SparseCore 0:
  131.3 104.0 all-reduce.5
